TPU v7x, 256 devices: a whole 4x4x8 slice. The times are simulated.
256 devices in a mesh: pipe: 8 (over z_hi, x), expert: 32 (over y, z_lo, core).
Axes of the slice: x: 4, y: 4, z: 8 (z_hi: 2, z_lo: 4; z = z_hi * 4 + z_lo), core: 2. Of those that a mesh axis runs over, the one named last changes fastest.
Arguments:
- grad_out: bfloat16 [8, 4096, 2048], P('pipe', 'expert'), may hold values from -6 to 6
- expert_ids: int32 [8, 4096, 8], P('pipe', 'expert'), may hold values from 0 to 63, as said below
- slot_ids: int32 [8, 4096, 8], P('pipe', 'expert'), may hold values from 0 to 16, as said below
- gate_weights: float32 [8, 4096, 8], P('pipe', 'expert'), may hold values from 0.02 to 0.6
- saved_pre: bfloat16 [8, 64, 512, 1536], P('pipe', 'expert'), may hold values from -6 to 6
- down_weight: bfloat16 [8, 64, 768, 2048], P('pipe', 'expert'), may hold values from -0.21875 to 0.21875
- router_weight: bfloat16 [8, 64, 2048], P('pipe', 'expert'), may hold values from -0.125 to 0.125
Outputs:
- pre_grad: bfloat16 [8, 64, 512, 1536], P('pipe', 'expert')
- grad_inputs: bfloat16 [8, 4096, 2048], P('pipe', 'expert')
Inputs may be any that keep to these rules, and one draw needn't show every extreme that they name: `expert_ids`: each row names 8 different experts. `slot_ids`: for the pair (t, k): the number of earlier pairs (by row, then by k) among the same device's 128 rows of that section that name the same expert, capped at 16; the value 16 marks a pair that is dropped.
All inputs are finite; a program needn't handle non-finite values.
Results may differ from a plain program's by a relative error of at most 0.012.
Values may be sent and summed in bfloat16 or wider, within the bound.
No kernel may reach another device: no remote copies, remote signals or barrier semaphores. Data moves between devices by JAX's collectives and lax.ppermute only.
A program may use at most 128 MiB of HBM per device.

v0:
```python
import jax
import jax.numpy as jnp
from jax import lax
from jax.sharding import PartitionSpec as P


def passed_along(value, axis, by):
    peers = lax.axis_size(axis)
    return lax.ppermute(value, axis, [(i, (i + by) % peers) for i in range(peers)])


def per_device(grad_out, expert_ids, slot_ids, gate_weights, saved_pre, down_weight, router_weight):
    groups = lax.axis_size("expert")
    local_experts = down_weight.shape[1]
    hidden_width = down_weight.shape[2]
    tok_rows = grad_out.shape[1]
    top_count = expert_ids.shape[2]
    expert_total = local_experts * groups
    capacity = tok_rows * top_count // expert_total
    total_rows = expert_total * capacity
    features = grad_out[0]
    route_ids = expert_ids[0]
    kept_pairs = slot_ids[0] < capacity
    destination = (
        route_ids % local_experts * (groups * capacity)
        + route_ids // local_experts * capacity
        + jnp.minimum(slot_ids[0], capacity - 1)
    )
    pair_dest = jnp.where(kept_pairs, destination, total_rows).reshape(-1)
    row_ids = jnp.arange(total_rows, dtype=jnp.int32)
    matches = pair_dest[None, :] == row_ids[:, None]
    pair_token = jnp.arange(tok_rows * top_count, dtype=jnp.int32) // top_count
    slot_token = jnp.sum(jnp.where(matches, pair_token[None, :], 0), axis=1)
    occupied = jnp.any(matches, axis=1)
    gate_low = gate_weights[0].astype(jnp.bfloat16)
    slot_gate = jnp.sum(
        jnp.where(matches, gate_low.reshape(-1).astype(jnp.float32)[None, :], jnp.float32(0.0)),
        axis=1,
    )
    token_rows = jnp.take(features, slot_token, axis=0)
    token_rows = jnp.where(occupied[:, None], token_rows, jnp.zeros_like(token_rows))
    pre_saved = saved_pre[0]
    gate_part = pre_saved[..., :hidden_width].astype(jnp.float32)
    up_part = pre_saved[..., hidden_width:].astype(jnp.float32)
    sigmoid_gate = jax.nn.sigmoid(gate_part)
    silu_gate = gate_part * sigmoid_gate
    hidden = (silu_gate * up_part).astype(jnp.bfloat16)
    weights = down_weight[0]
    expert_out = jnp.einsum(
        "jsf,jfd->jsd", hidden, weights, preferred_element_type=jnp.float32
    ).astype(jnp.bfloat16)
    scaled = (slot_gate[:, None] * token_rows.astype(jnp.float32)).astype(jnp.bfloat16)
    arrived = lax.all_to_all(
        scaled.reshape(local_experts, groups, capacity, -1),
        "expert",
        split_axis=1,
        concat_axis=1,
        tiled=True,
    )
    scaled_rows = arrived.reshape(local_experts, groups * capacity, -1)
    returned = lax.all_to_all(
        expert_out.reshape(local_experts, groups, capacity, -1),
        "expert",
        split_axis=1,
        concat_axis=1,
        tiled=True,
    )
    pair_out = jnp.take(
        returned.reshape(total_rows, -1), pair_dest, axis=0, mode="fill", fill_value=0
    )
    pair_scores = jnp.sum(
        pair_out.reshape(tok_rows, top_count, -1).astype(jnp.float32)
        * features.astype(jnp.float32)[:, None, :],
        axis=-1,
    )
    row_grad = jnp.einsum("jsd,jfd->jsf", scaled_rows, weights, preferred_element_type=jnp.float32)
    gate_grad = row_grad * up_part * sigmoid_gate * (1.0 + gate_part * (1.0 - sigmoid_gate))
    up_grad = row_grad * silu_gate
    pre_grad = jnp.concatenate([gate_grad, up_grad], axis=-1).astype(jnp.bfloat16)
    gate_values = gate_weights[0]
    weighted_sum = jnp.sum(gate_values * pair_scores, axis=-1, keepdims=True)
    select_grad = gate_values * (pair_scores - weighted_sum)
    expert_columns = jnp.arange(expert_total, dtype=jnp.int32)
    chosen = route_ids[:, :, None] == expert_columns[None, None, :]
    logit_grad = jnp.sum(
        jnp.where(chosen, select_grad[:, :, None], jnp.float32(0.0)), axis=1
    ).astype(jnp.bfloat16)
    router_part = jnp.dot(
        logit_grad,
        lax.all_gather(router_weight[0], "expert", axis=0, tiled=True),
        preferred_element_type=jnp.float32,
    )
    section_grad = (features.astype(jnp.float32) + router_part).astype(jnp.bfloat16)
    outgoing = passed_along(section_grad, "pipe", -1)
    return (pre_grad[None], outgoing[None])


def solution(mesh):
    in_specs = (
        P("pipe", "expert", None),
        P("pipe", "expert", None),
        P("pipe", "expert", None),
        P("pipe", "expert", None),
        P("pipe", "expert", None, None),
        P("pipe", "expert", None, None),
        P("pipe", "expert", None),
    )
    out_specs = (P("pipe", "expert", None, None), P("pipe", "expert", None))
    return jax.shard_map(
        per_device, mesh=mesh, in_specs=in_specs, out_specs=out_specs, check_vma=False
    )
```

profile of v0, /device:TPU:7, one launch (start us, length us, event | category | flops | bytes accessed | tf_op | source)
XLA Modules:
  0.0 298.4 jit_solution(13683775158880791183)
XLA Ops:
  0.6 7.4 %fusion.7 = bf16[2,512,2048]{2,1,0:T(8,128)(2,1)S(1)} fusion(bf16[1,2,768,2048]{3,2,1,0:T(8,128)(2,1)} %param.12, bf16[2,512,1536]{2,1,0:T(8,128)(2,1)} %bitcast.59), kind=kOutput, calls=%fused_computation.20 | convolution fusion | flops 3229614080 | bytes 13631488 | tf_op jit(solution)/shard_map/jsf,jfd->jsd/dot_general | solution.py:49
  8.0 2.3 copy.68
  10.3 9.6 %all-to-all-start.1 = ((bf16[2,32,16,2048]{3,2,0,1:T(8,128)(2,1)}), bf16[2,32,16,2048]{3,2,0,1:T(8,128)(2,1)}, u32[]{:S(2)}, u32[]{:S(2)}) async-start(bf16[2,32,16,2048]{3,2,0,1:T(8,128)(2,1)} %copy.68), calls=%async_computation.1 | async-start | bytes 8388608 | tf_op jit(solution)/shard_map/all_to_all | solution.py:61
  20.0 0.1 copy.57
  20.5 0.5 select_reduce_fusion
  21.4 0.5 select_reduce_fusion.1
  22.0 0.6 fusion.6
  22.7 6.0 %gather_fusion = bf16[1024,2048]{1,0:T(8,128)(2,1)} fusion(bf16[128,2048]{1,0:T(8,128)(2,1)S(1)} %bitcast.49, s32[1024]{0:T(1024)S(1)} %broadcast_clamp_fusion.1), kind=kCustom, calls=%fused_computation | custom fusion | bytes 8392704 | tf_op jit(solution)/shard_map/jit(_take)/gather | solution.py:40
  28.7 4.5 %multiply_convert_fusion = bf16[2,32,16,2048]{3,2,0,1:T(8,128)(2,1)} fusion(bf16[2,32,16,2048]{3,2,1,0:T(8,128)(2,1)} %bitcast.51, f32[2,32,16]{2,0,1:T(2,128)S(1)} %copy.61, pred[2,32,16]{2,0,1:T(4,128)(4,1)S(1)} %copy.63, pred[2,32,16]{2,0,1:T(4,128)(4,1)S(1)} %copy.62), kind=kLoop, calls=%fused_computation.4 | loop fusion | flops 10485760 | bytes 8394752 | tf_op jit(solution)/shard_map/convert_element_type | solution.py:52
  33.3 81.1 %all-to-all-done.1 = bf16[2,32,16,2048]{3,2,0,1:T(8,128)(2,1)} async-done(((bf16[2,32,16,2048]{3,2,0,1:T(8,128)(2,1)}), bf16[2,32,16,2048]{3,2,0,1:T(8,128)(2,1)}, u32[]{:S(2)}, u32[]{:S(2)}) %all-to-all-start.1) | async-done | bytes 4194336 | tf_op jit(solution)/shard_map/all_to_all | solution.py:61
  114.4 5.5 %all-to-all-start = ((bf16[2,32,16,2048]{3,2,0,1:T(8,128)(2,1)}), bf16[2,32,16,2048]{3,2,0,1:T(8,128)(2,1)}, u32[]{:S(2)}, u32[]{:S(2)}) async-start(bf16[2,32,16,2048]{3,2,0,1:T(8,128)(2,1)} %multiply_convert_fusion), calls=%async_computation | async-start | bytes 8388608 | tf_op jit(solution)/shard_map/all_to_all | solution.py:53
  120.3 0.1 copy.67
  120.6 126.3 %all-gather = bf16[1,64,2048]{2,0,1:T(2,128)(2,1)S(1)} all-gather(bf16[1,2,2048]{2,0,1:T(2,128)(2,1)S(1)} %copy.74), channel_id=2, replica_groups=mesh['pipe'=8,'expert'=32] {'expert'}, dimensions={1}, use_global_device_ids=true | all-gather | bytes 270336 | tf_op jit(solution)/shard_map/all_gather | solution.py:90
  247.0 4.7 %copy.69 = bf16[2,32,16,2048]{3,2,1,0:T(8,128)(2,1)} copy(bf16[2,32,16,2048]{3,2,0,1:T(8,128)(2,1)} %all-to-all-done.1) | data formatting | bytes 8388608 | tf_op jit(solution)/shard_map/all_to_all | solution.py:61
  251.8 11.6 %gather_fusion.1 = bf16[1024,2048]{1,0:T(8,128)(2,1)} fusion(bf16[1024,2048]{1,0:T(8,128)(2,1)} %bitcast.50, s32[1024]{0:T(1024)S(1)} %broadcast_clamp_fusion), kind=kCustom, calls=%fused_computation.1 | custom fusion | bytes 8392704 | tf_op jit(solution)/shard_map/jit(_take)/gather | solution.py:68
  263.3 3.2 %fusion = f32[1024]{0:T(1024)S(1)} fusion(f32[128,2048]{1,0:T(8,128)S(1)} %bitcast_convert_fusion, bf16[1024,2048]{1,0:T(8,128)(2,1)} %gather_fusion.1, pred[1024]{0:T(1024)(128)(4,1)S(1)} %broadcast_in_dim.103), kind=kLoop, calls=%fused_computation.3 | loop fusion | flops 8387584 | bytes 5248000 | tf_op jit(solution)/shard_map/reduce_sum | solution.py:71
  267.0 0.3 fusion.18
  267.3 0.8 collective-permute-start
  268.1 2.7 copy.65
  270.8 0.5 copy-done.5
  271.3 7.3 %fusion.21 = (bf16[1,2,512,768]{3,2,1,0:T(8,128)(2,1)S(1)}, bf16[1,2,512,768]{3,2,1,0:T(8,128)(2,1)S(1)}) fusion(bf16[2,512,1536]{2,1,0:T(8,128)(2,1)S(1)} %bitcast.60, bf16[2,512,2048]{2,1,0:T(8,128)(2,1)S(1)} %bitcast.52, bf16[1,2,768,2048]{3,2,1,0:T(8,128)(2,1)} %param.12), kind=kOutput, calls=%fused_computation.34 | convolution fusion | flops 3233021952 | bytes 16777216 | tf_op jit(solution)/shard_map/jsd,jfd->jsf/dot_general | solution.py:76
  278.5 1.9 pad_maximum_fusion
  280.5 17.2 %collective-permute-done = bf16[128,2048]{1,0:T(8,128)(2,1)S(1)} collective-permute-done((bf16[128,2048]{1,0:T(8,128)(2,1)S(1)}, bf16[128,2048]{1,0:T(8,128)(2,1)S(1)}, u32[]{:S(2)}, u32[]{:S(2)}) %collective-permute-start) | collective-permute-done | bytes 524320 | tf_op jit(solution)/shard_map/ppermute | solution.py:9
  297.6 0.8 copy.86
  (46 shorter events, 2.1 us)
Async XLA Ops:
  10.3 9.6 %copy-start.1 = (s32[1,128,8]{1,2,0:T(8,128)S(1)}, s32[1,128,8]{1,2,0:T(8,128)}, u32[]{:S(2)}) copy-start(s32[1,128,8]{1,2,0:T(8,128)} %param.8) | copy-start | bytes 12292
  10.3 9.7 %copy-start.3 = (s32[1,128,8]{1,2,0:T(8,128)S(1)}, s32[1,128,8]{1,2,0:T(8,128)}, u32[]{:S(2)}) copy-start(s32[1,128,8]{1,2,0:T(8,128)} %param.9) | copy-start | bytes 12292
  10.3 10.9 %copy-start.2 = (f32[1,128,8]{1,2,0:T(8,128)S(1)}, f32[1,128,8]{1,2,0:T(8,128)}, u32[]{:S(2)}) copy-start(f32[1,128,8]{1,2,0:T(8,128)} %param.10) | copy-start | bytes 12292
  10.3 12.4 %copy-start = (bf16[1,128,2048]{2,1,0:T(8,128)(2,1)S(1)}, bf16[1,128,2048]{2,1,0:T(8,128)(2,1)}, u32[]{:S(2)}) copy-start(bf16[1,128,2048]{2,1,0:T(8,128)(2,1)} %param.7) | copy-start | bytes 1572868
  10.3 104.1 %all-to-all-start.1 = ((bf16[2,32,16,2048]{3,2,0,1:T(8,128)(2,1)}), bf16[2,32,16,2048]{3,2,0,1:T(8,128)(2,1)}, u32[]{:S(2)}, u32[]{:S(2)}) async-start(bf16[2,32,16,2048]{3,2,0,1:T(8,128)(2,1)} %copy.68), calls=%async_computation.1 | async-start | bytes 8388608 | tf_op jit(solution)/shard_map/all_to_all | solution.py:61
  33.3 87.3 %copy-start.4 = (bf16[1,2,2048]{2,1,0:T(2,128)(2,1)S(1)}, bf16[1,2,2048]{2,1,0:T(2,128)(2,1)}, u32[]{:S(2)}) copy-start(bf16[1,2,2048]{2,1,0:T(2,128)(2,1)} %param.13) | copy-start | bytes 24580
  114.4 153.7 %all-to-all-start = ((bf16[2,32,16,2048]{3,2,0,1:T(8,128)(2,1)}), bf16[2,32,16,2048]{3,2,0,1:T(8,128)(2,1)}, u32[]{:S(2)}, u32[]{:S(2)}) async-start(bf16[2,32,16,2048]{3,2,0,1:T(8,128)(2,1)} %multiply_convert_fusion), calls=%async_computation | async-start | bytes 8388608 | tf_op jit(solution)/shard_map/all_to_all | solution.py:53
  267.3 30.3 %collective-permute-start = (bf16[128,2048]{1,0:T(8,128)(2,1)S(1)}, bf16[128,2048]{1,0:T(8,128)(2,1)S(1)}, u32[]{:S(2)}, u32[]{:S(2)}) collective-permute-start(bf16[128,2048]{1,0:T(8,128)(2,1)S(1)} %fusion.18), channel_id=1, source_target_pairs={{0,224},{32,0},{64,32},{96,64},{128,96},{160,128},{192,160},{224,1... | collective-permute-start | bytes 1572872 | tf_op jit(solution)/shard_map/ppermute | solution.py:9
  268.1 3.2 %copy-start.5 = (bf16[1,2,512,1536]{3,2,1,0:T(8,128)(2,1)S(1)}, bf16[1,2,512,1536]{3,2,1,0:T(8,128)(2,1)}, u32[]{:S(2)}) copy-start(bf16[1,2,512,1536]{3,2,1,0:T(8,128)(2,1)} %param.11) | copy-start | bytes 9437188
where the time goes:
time: 299 us; the launch traced here: 298 us
  blocking collectives  126 us (42%)
  waiting for transfers between devices  98.3 us (33%)
  local copies, waits for them, and re-layouts  30.4 us (10%)
  starting transfers between devices  15.9 us (5%)
  matrix products  15 us (5%)
  other arithmetic  11.7 us (4%)
    all_gather x1, blocking collectives, per_device(): lax.all_gather(router_weight[0], 'expert', axis=0, tiled=True)  126 us
    all_to_all x1, waiting for transfers between devices, per_device(): lax.all_to_all(expert_out.reshape(local_experts, groups, capacity, -1), '...  81.1 us
    ppermute x1, waiting for transfers between devices, passed_along(): lax.ppermute(value, axis, [(i, (i + by) % peers) for i in range(peers)])  17.2 us
    gather x1, local copies, waits for them, and re-layouts, per_device(): jnp.take(returned.reshape(total_rows, -1), pair_dest, axis=0, mode='fill'...  11.6 us
    all_to_all x1, starting transfers between devices, per_device(): lax.all_to_all(expert_out.reshape(local_experts, groups, capacity, -1), '...  9.56 us
    dot_general x1, matrix products, per_device(): jnp.einsum('jsf,jfd->jsd', hidden, weights, preferred_element_type=jnp.fl...  7.37 us
    dot_general x1, matrix products, per_device(): jnp.einsum('jsd,jfd->jsf', scaled_rows, weights, preferred_element_type=j...  7.27 us
    gather x1, local copies, waits for them, and re-layouts, per_device(): token_rows = jnp.take(features, slot_token, axis=0)  6.02 us
  transfers between devices with their start and end apart: 3, of which 2 were waited for; matrix products, arithmetic and copies ran while one was open for 15% of the time, Pallas kernels for 0%

commit v1 on v0

--- a/solution.py
+++ b/solution.py
@@ -1,7 +1,21 @@
+import functools
 import jax
 import jax.numpy as jnp
 from jax import lax
 from jax.sharding import PartitionSpec as P
+
+
+def draft_marks(buf, peer_axis):
+    z = lax.all_to_all(
+        jnp.stack([buf] * lax.psum(1, axis_name=peer_axis)),
+        axis_name=peer_axis,
+        split_axis=0,
+        concat_axis=0,
+    )
+    return jnp.concatenate(z, 0)
+
+
+_get_gates = functools.partial(draft_marks, peer_axis="expert")
 
 
 def passed_along(value, axis, by):
@@ -86,9 +100,7 @@
         jnp.where(chosen, select_grad[:, :, None], jnp.float32(0.0)), axis=1
     ).astype(jnp.bfloat16)
     router_part = jnp.dot(
-        logit_grad,
-        lax.all_gather(router_weight[0], "expert", axis=0, tiled=True),
-        preferred_element_type=jnp.float32,
+        logit_grad, _get_gates(router_weight[0]), preferred_element_type=jnp.float32
     )
     section_grad = (features.astype(jnp.float32) + router_part).astype(jnp.bfloat16)
     outgoing = passed_along(section_grad, "pipe", -1)

time: 299 us -> 261 us (0.87)
  the two profiles are of different devices: /device:TPU:7 before, /device:TPU:1 now
where the time goes in v1:
time: 261 us; the launch traced here: 260 us
  waiting for transfers between devices  172 us (66%)
  local copies, waits for them, and re-layouts  32 us (12%)
  starting transfers between devices  28.6 us (11%)
  matrix products  15 us (6%)
  other arithmetic  11.7 us (4%)
    all_to_all x1, waiting for transfers between devices, per_device(): lax.all_to_all(scaled.reshape(local_experts, groups, capacity, -1), 'expe...  89.2 us
    all_to_all x1, waiting for transfers between devices, per_device(): lax.all_to_all(expert_out.reshape(local_experts, groups, capacity, -1), '...  81.1 us
    gather x1, local copies, waits for them, and re-layouts, per_device(): jnp.take(returned.reshape(total_rows, -1), pair_dest, axis=0, mode='fill'...  11.6 us
    all_to_all x1, starting transfers between devices, draft_marks(): lax.all_to_all(jnp.stack([buf] * lax.psum(1, axis_name=peer_axis)), axis_...  10.2 us
    dot_general x1, matrix products, per_device(): jnp.einsum('jsf,jfd->jsd', hidden, weights, preferred_element_type=jnp.fl...  7.37 us
    dot_general x1, matrix products, per_device(): jnp.einsum('jsd,jfd->jsf', scaled_rows, weights, preferred_element_type=j...  7.27 us
    ppermute x1, starting transfers between devices, passed_along(): lax.ppermute(value, axis, [(i, (i + by) % peers) for i in range(peers)])  6.66 us
    all_to_all x1, starting transfers between devices, per_device(): lax.all_to_all(expert_out.reshape(local_experts, groups, capacity, -1), '...  6.31 us
  transfers between devices with their start and end apart: 4, of which 3 were waited for; matrix products, arithmetic and copies ran while one was open for 21% of the time, Pallas kernels for 0%

profile of v1, /device:TPU:1, one launch (start us, length us, event | category | flops | bytes accessed | tf_op | source)
XLA Modules:
  0.0 260.1 jit_solution(5292674042120520201)
XLA Ops:
  0.6 1.5 stack.3
  2.2 10.2 %all-to-all-start.2 = ((bf16[32,2,2048]{2,1,0:T(2,128)(2,1)}), bf16[32,2,2048]{2,1,0:T(2,128)(2,1)S(1)}, u32[]{:S(2)}, u32[]{:S(2)}) async-start(bf16[32,2,2048]{2,1,0:T(2,128)(2,1)} %stack.3), calls=%async_computation.2 | async-start | bytes 524288 | tf_op jit(solution)/shard_map/all_to_all | solution.py:9
  12.4 7.4 %fusion.7 = bf16[2,512,2048]{2,1,0:T(8,128)(2,1)S(1)} fusion(bf16[1,2,768,2048]{3,2,1,0:T(8,128)(2,1)} %param.12, bf16[2,512,1536]{2,1,0:T(8,128)(2,1)} %bitcast.59), kind=kOutput, calls=%fused_computation.20 | convolution fusion | flops 3229614080 | bytes 13631488 | tf_op jit(solution)/shard_map/jsf,jfd->jsd/dot_general | solution.py:63
  19.7 2.3 copy.49
  22.0 1.6 all-to-all-done.2
  23.6 6.3 %all-to-all-start.1 = ((bf16[2,32,16,2048]{3,2,0,1:T(8,128)(2,1)}), bf16[2,32,16,2048]{3,2,0,1:T(8,128)(2,1)}, u32[]{:S(2)}, u32[]{:S(2)}) async-start(bf16[2,32,16,2048]{3,2,0,1:T(8,128)(2,1)} %copy.49), calls=%async_computation.1 | async-start | bytes 8388608 | tf_op jit(solution)/shard_map/all_to_all | solution.py:75
  30.6 0.5 select_reduce_fusion
  31.4 0.5 select_reduce_fusion.1
  32.1 0.6 fusion.6
  32.8 6.0 %gather_fusion = bf16[1024,2048]{1,0:T(8,128)(2,1)} fusion(bf16[128,2048]{1,0:T(8,128)(2,1)S(1)} %bitcast.48, s32[1024]{0:T(1024)S(1)} %broadcast_clamp_fusion.1), kind=kCustom, calls=%fused_computation | custom fusion | bytes 8392704 | tf_op jit(solution)/shard_map/jit(_take)/gather | solution.py:54
  38.8 4.5 %multiply_convert_fusion = bf16[2,32,16,2048]{3,2,0,1:T(8,128)(2,1)} fusion(bf16[2,32,16,2048]{3,2,1,0:T(8,128)(2,1)} %bitcast.50, f32[2,32,16]{2,0,1:T(2,128)S(1)} %copy.42, pred[2,32,16]{2,0,1:T(4,128)(4,1)S(1)} %copy.44, pred[2,32,16]{2,0,1:T(4,128)(4,1)S(1)} %copy.43), kind=kLoop, calls=%fused_computation.4 | loop fusion | flops 10485760 | bytes 8394752 | tf_op jit(solution)/shard_map/convert_element_type | solution.py:66
  43.3 81.1 %all-to-all-done.1 = bf16[2,32,16,2048]{3,2,0,1:T(8,128)(2,1)} async-done(((bf16[2,32,16,2048]{3,2,0,1:T(8,128)(2,1)}), bf16[2,32,16,2048]{3,2,0,1:T(8,128)(2,1)}, u32[]{:S(2)}, u32[]{:S(2)}) %all-to-all-start.1) | async-done | bytes 4194336 | tf_op jit(solution)/shard_map/all_to_all | solution.py:75
  124.4 5.5 %all-to-all-start = ((bf16[2,32,16,2048]{3,2,0,1:T(8,128)(2,1)}), bf16[2,32,16,2048]{3,2,0,1:T(8,128)(2,1)}, u32[]{:S(2)}, u32[]{:S(2)}) async-start(bf16[2,32,16,2048]{3,2,0,1:T(8,128)(2,1)} %multiply_convert_fusion), calls=%async_computation | async-start | bytes 8388608 | tf_op jit(solution)/shard_map/all_to_all | solution.py:67
  130.8 4.7 %copy.50 = bf16[2,32,16,2048]{3,2,1,0:T(8,128)(2,1)} copy(bf16[2,32,16,2048]{3,2,0,1:T(8,128)(2,1)} %all-to-all-done.1) | data formatting | bytes 8388608 | tf_op jit(solution)/shard_map/all_to_all | solution.py:75
  135.6 11.6 %gather_fusion.1 = bf16[1024,2048]{1,0:T(8,128)(2,1)} fusion(bf16[1024,2048]{1,0:T(8,128)(2,1)} %bitcast.49, s32[1024]{0:T(1024)S(1)} %broadcast_clamp_fusion), kind=kCustom, calls=%fused_computation.1 | custom fusion | bytes 8392704 | tf_op jit(solution)/shard_map/jit(_take)/gather | solution.py:82
  147.1 3.2 %fusion = f32[1024]{0:T(1024)S(1)} fusion(f32[128,2048]{1,0:T(8,128)S(1)} %bitcast_convert_fusion, bf16[1024,2048]{1,0:T(8,128)(2,1)} %gather_fusion.1, pred[1024]{0:T(1024)(128)(4,1)S(1)} %broadcast_in_dim.103), kind=kLoop, calls=%fused_computation.3 | loop fusion | flops 8387584 | bytes 5248000 | tf_op jit(solution)/shard_map/reduce_sum | solution.py:85
  150.8 0.3 fusion.18
  151.1 6.7 %collective-permute-start = (bf16[128,2048]{1,0:T(8,128)(2,1)S(1)}, bf16[128,2048]{1,0:T(8,128)(2,1)S(1)}, u32[]{:S(2)}, u32[]{:S(2)}) collective-permute-start(bf16[128,2048]{1,0:T(8,128)(2,1)S(1)} %fusion.18), channel_id=1, source_target_pairs={{0,224},{32,0},{64,32},{96,64},{128,96},{160,128},{192,160},{224,1... | collective-permute-start | bytes 1572872 | tf_op jit(solution)/shard_map/ppermute | solution.py:23
  157.8 89.2 %all-to-all-done = bf16[2,32,16,2048]{3,2,0,1:T(8,128)(2,1)} async-done(((bf16[2,32,16,2048]{3,2,0,1:T(8,128)(2,1)}), bf16[2,32,16,2048]{3,2,0,1:T(8,128)(2,1)}, u32[]{:S(2)}, u32[]{:S(2)}) %all-to-all-start) | async-done | bytes 4194336 | tf_op jit(solution)/shard_map/all_to_all | solution.py:67
  247.0 2.7 %copy.46 = bf16[2,32,16,2048]{3,2,1,0:T(8,128)(2,1)S(1)} copy(bf16[2,32,16,2048]{3,2,0,1:T(8,128)(2,1)} %all-to-all-done) | data formatting | bytes 8388608 | tf_op jit(solution)/shard_map/all_to_all | solution.py:67
  249.7 0.5 copy-done.4
  250.2 7.3 %fusion.21 = (bf16[1,2,512,768]{3,2,1,0:T(8,128)(2,1)S(1)}, bf16[1,2,512,768]{3,2,1,0:T(8,128)(2,1)S(1)}) fusion(bf16[2,512,1536]{2,1,0:T(8,128)(2,1)S(1)} %bitcast.60, bf16[2,512,2048]{2,1,0:T(8,128)(2,1)S(1)} %bitcast.51, bf16[1,2,768,2048]{3,2,1,0:T(8,128)(2,1)} %param.12), kind=kOutput, calls=%fused_computation.34 | convolution fusion | flops 3233021952 | bytes 16777216 | tf_op jit(solution)/shard_map/jsd,jfd->jsf/dot_general | solution.py:90
  257.4 1.9 pad_maximum_fusion
  259.3 0.8 copy.61
  (46 shorter events, 2.5 us)
Async XLA Ops:
  2.2 21.4 %all-to-all-start.2 = ((bf16[32,2,2048]{2,1,0:T(2,128)(2,1)}), bf16[32,2,2048]{2,1,0:T(2,128)(2,1)S(1)}, u32[]{:S(2)}, u32[]{:S(2)}) async-start(bf16[32,2,2048]{2,1,0:T(2,128)(2,1)} %stack.3), calls=%async_computation.2 | async-start | bytes 524288 | tf_op jit(solution)/shard_map/all_to_all | solution.py:9
  22.0 7.9 %copy-start.1 = (s32[1,128,8]{1,2,0:T(8,128)S(1)}, s32[1,128,8]{1,2,0:T(8,128)}, u32[]{:S(2)}) copy-start(s32[1,128,8]{1,2,0:T(8,128)} %param.8) | copy-start | bytes 12292
  22.0 8.0 %copy-start.3 = (s32[1,128,8]{1,2,0:T(8,128)S(1)}, s32[1,128,8]{1,2,0:T(8,128)}, u32[]{:S(2)}) copy-start(s32[1,128,8]{1,2,0:T(8,128)} %param.9) | copy-start | bytes 12292
  22.0 9.2 %copy-start.2 = (f32[1,128,8]{1,2,0:T(8,128)S(1)}, f32[1,128,8]{1,2,0:T(8,128)}, u32[]{:S(2)}) copy-start(f32[1,128,8]{1,2,0:T(8,128)} %param.10) | copy-start | bytes 12292
  22.0 10.7 %copy-start = (bf16[1,128,2048]{2,1,0:T(8,128)(2,1)S(1)}, bf16[1,128,2048]{2,1,0:T(8,128)(2,1)}, u32[]{:S(2)}) copy-start(bf16[1,128,2048]{2,1,0:T(8,128)(2,1)} %param.7) | copy-start | bytes 1572868
  23.6 100.8 %all-to-all-start.1 = ((bf16[2,32,16,2048]{3,2,0,1:T(8,128)(2,1)}), bf16[2,32,16,2048]{3,2,0,1:T(8,128)(2,1)}, u32[]{:S(2)}, u32[]{:S(2)}) async-start(bf16[2,32,16,2048]{3,2,0,1:T(8,128)(2,1)} %copy.49), calls=%async_computation.1 | async-start | bytes 8388608 | tf_op jit(solution)/shard_map/all_to_all | solution.py:75
  124.4 122.6 %all-to-all-start = ((bf16[2,32,16,2048]{3,2,0,1:T(8,128)(2,1)}), bf16[2,32,16,2048]{3,2,0,1:T(8,128)(2,1)}, u32[]{:S(2)}, u32[]{:S(2)}) async-start(bf16[2,32,16,2048]{3,2,0,1:T(8,128)(2,1)} %multiply_convert_fusion), calls=%async_computation | async-start | bytes 8388608 | tf_op jit(solution)/shard_map/all_to_all | solution.py:67
  151.1 108.2 %collective-permute-start = (bf16[128,2048]{1,0:T(8,128)(2,1)S(1)}, bf16[128,2048]{1,0:T(8,128)(2,1)S(1)}, u32[]{:S(2)}, u32[]{:S(2)}) collective-permute-start(bf16[128,2048]{1,0:T(8,128)(2,1)S(1)} %fusion.18), channel_id=1, source_target_pairs={{0,224},{32,0},{64,32},{96,64},{128,96},{160,128},{192,160},{224,1... | collective-permute-start | bytes 1572872 | tf_op jit(solution)/shard_map/ppermute | solution.py:23
  247.0 3.2 %copy-start.4 = (bf16[1,2,512,1536]{3,2,1,0:T(8,128)(2,1)S(1)}, bf16[1,2,512,1536]{3,2,1,0:T(8,128)(2,1)}, u32[]{:S(2)}) copy-start(bf16[1,2,512,1536]{3,2,1,0:T(8,128)(2,1)} %param.11) | copy-start | bytes 9437188
